TPU v7x, 32 devices: a whole 2x2x4 slice. The times are simulated.
32 devices in a mesh: dp: 16 (over z, x, core), group: 2 (over y).
Axes of the slice: x: 2, y: 2, z: 4, core: 2. Of those that a mesh axis runs over, the one named last changes fastest.
Arguments:
- inputs: bfloat16 [32768, 2048], P('dp', 'group'), may hold values from -6 to 6
- grad_out: bfloat16 [32768, 2048], P(('dp', 'group')), may hold values from -0.0625 to 0.0625
- weight: bfloat16 [2048, 2048], P('group'), may hold values from -6 to 6
- old_basis: float32 [2048, 256], P('group'), may hold values from -0.125 to 0.125
- first_moment: float32 [256, 2048], P(None, 'dp'), may hold values from -6 to 6
- second_moment: float32 [256, 2048], P(None, 'dp'), may hold values from 0.1 to 3
Outputs:
- new_weight: bfloat16 [2048, 2048], P('group')
- new_first: float32 [256, 2048], P(None, 'dp')
- new_second: float32 [256, 2048], P(None, 'dp')
- new_basis: float32 [2048, 256], P('group')
All inputs are finite; a program needn't handle non-finite values.
Results may differ from a plain program's by a relative error of at most 0.011.
Values may be sent and summed in bfloat16 or wider, within the bound.
No kernel may reach another device: no remote copies, remote signals or barrier semaphores. Data moves between devices by JAX's collectives and lax.ppermute only.
A program may use at most 64 MiB of HBM per device.

v0:
```python
import jax
import jax.numpy as jnp
from jax import lax
from jax.sharding import PartitionSpec as P

NS_STEPS = 5
STEP = 10
BETA_ONE = 0.9
BETA_TWO = 0.99
ADAM_EPS = 1e-08
HIGHEST = lax.Precision.HIGHEST


def matmul(left, right):
    return jnp.dot(left, right, precision=HIGHEST)


def inner_gram(matrix):
    return lax.dot_general(matrix, matrix, (((0,), (0,)), ((), ())), precision=HIGHEST)


def refine_group(subspace):
    squares = lax.psum(jnp.sum(subspace * subspace), "group")
    iterate = subspace / jnp.sqrt(squares)
    for sweep in range(NS_STEPS):
        gram = lax.psum(inner_gram(iterate).astype(jnp.bfloat16), "group").astype(jnp.float32)
        iterate = 1.5 * iterate - 0.5 * matmul(iterate, gram)
    return iterate


def shards(inputs, grad_out, weight, old_basis, first_moment, second_moment):
    partial_grad = lax.dot_general(
        inputs,
        lax.all_gather(grad_out, "group", axis=0, tiled=True),
        (((0,), (0,)), ((), ())),
        preferred_element_type=jnp.float32,
    )
    grad_block = lax.psum_scatter(partial_grad, "dp", scatter_dimension=1, tiled=True)
    projected = lax.psum(matmul(old_basis.T, grad_block).astype(jnp.bfloat16), "group").astype(
        jnp.float32
    )
    new_first = BETA_ONE * first_moment + (1.0 - BETA_ONE) * projected
    new_second = BETA_TWO * second_moment + (1.0 - BETA_TWO) * projected * projected
    direction = (
        new_first
        / (1.0 - BETA_ONE**STEP)
        / (jnp.sqrt(new_second / (1.0 - BETA_TWO**STEP)) + ADAM_EPS)
    )
    col_count = grad_block.shape[1]
    col_offset = lax.axis_index("dp") * col_count
    own_cols = lax.dynamic_slice_in_dim(weight, col_offset, col_count, 1).astype(jnp.float32)
    updated = (own_cols - matmul(old_basis, direction)).astype(jnp.bfloat16)
    new_weight = lax.all_gather(updated, "dp", axis=1, tiled=True)
    subspace_terms = matmul(grad_block, projected.T)
    subspace = lax.psum(subspace_terms, "dp")
    new_basis = refine_group(subspace)
    return (new_weight, new_first, new_second, new_basis)


def solution(mesh):
    return jax.shard_map(
        shards,
        mesh=mesh,
        in_specs=(
            P("dp", "group"),
            P(("dp", "group"), None),
            P("group", None),
            P("group", None),
            P(None, "dp"),
            P(None, "dp"),
        ),
        out_specs=(P("group", None), P(None, "dp"), P(None, "dp"), P("group", None)),
        check_vma=False,
    )
```

profile of v0, /device:TPU:0, one launch (start us, length us, event | category | flops | bytes accessed | tf_op | source)
XLA Modules:
  0.0 558.3 jit_solution(406713574473706663)
XLA Ops:
  8.0 108.3 %all-gather.3.cloned.1.call-done = bf16[2048,2048]{1,0:T(8,128)(2,1)} async-done(((bf16[1024,2048]{1,0:T(8,128)(2,1)}), bf16[2048,2048]{1,0:T(8,128)(2,1)}) %all-gather.3.cloned.1.call-update) | async-done | bytes 8388624 | tf_op jit(solution)/shard_map/all_gather | solution.py:34
  116.3 14.6 %fusion.21 = f32[1024,2048]{1,0:T(8,128)} fusion(bf16[2048,1024]{1,0:T(8,128)(2,1)} %param.6, bf16[2048,2048]{1,0:T(8,128)(2,1)} %all-gather.3.cloned.1.call-done), kind=kOutput, calls=%fused_computation.38 | convolution fusion | flops 8589934592 | bytes 20971520 | tf_op jit(solution)/shard_map/dot_general | solution.py:32
  130.9 103.7 %reduce-scatter.2.cloned.1.call-done = f32[1024,128]{1,0:T(8,128)} async-done(((f32[1024,2048]{1,0:T(8,128)}), f32[1024,128]{1,0:T(8,128)}) %reduce-scatter.2.cloned.1.call-update) | async-done | bytes 524304 | tf_op jit(solution)/shard_map/reduce_scatter | solution.py:38
  234.6 2.7 fusion.7
  237.4 20.7 %all-reduce.8.cloned.1.call-done = bf16[256,128]{0,1:T(8,128)(2,1)} async-done(((bf16[256,128]{0,1:T(8,128)(2,1)}), bf16[256,128]{0,1:T(8,128)(2,1)}) %all-reduce.8.cloned.1.call-update) | async-done | bytes 65552 | tf_op jit(solution)/shard_map/psum | solution.py:39
  258.1 2.6 fusion.22
  260.8 95.1 %all-reduce.10.cloned.1.call-done = f32[1024,256]{1,0:T(8,128)} async-done(((f32[1024,256]{1,0:T(8,128)}), f32[1024,256]{1,0:T(8,128)}) %all-reduce.10.cloned.1.call-update) | async-done | bytes 1048592 | tf_op jit(solution)/shard_map/psum | solution.py:55
  355.8 2.2 multiply_reduce_fusion
  358.0 5.5 psum.58
  364.3 4.0 convolution_convert_fusion.4
  368.4 20.7 %all-reduce.12.cloned.1.call-done = bf16[256,256]{1,0:T(8,128)(2,1)} async-done(((bf16[256,256]{1,0:T(8,128)(2,1)}), bf16[256,256]{1,0:T(8,128)(2,1)}) %all-reduce.12.cloned.1.call-update) | async-done | bytes 131088 | tf_op jit(solution)/shard_map/psum | solution.py:26
  389.1 1.6 fusion.4
  390.7 2.5 convolution_convert_fusion.3
  393.5 21.4 %all-reduce.14.cloned.1.call-done = bf16[256,256]{1,0:T(8,128)(2,1)} async-done(((bf16[256,256]{1,0:T(8,128)(2,1)}), bf16[256,256]{1,0:T(8,128)(2,1)}) %all-reduce.14.cloned.1.call-update) | async-done | bytes 131088 | tf_op jit(solution)/shard_map/psum | solution.py:26
  414.9 1.5 fusion.3
  416.4 2.5 convolution_convert_fusion.2
  419.0 1.0 constant_dynamic-slice_fusion
  420.0 0.9 copy.16
  421.0 0.8 copy.12
  421.7 18.9 %all-reduce.16.cloned.1.call-done = bf16[256,256]{1,0:T(8,128)(2,1)} async-done(((bf16[256,256]{1,0:T(8,128)(2,1)}), bf16[256,256]{1,0:T(8,128)(2,1)}) %all-reduce.16.cloned.1.call-update) | async-done | bytes 131088 | tf_op jit(solution)/shard_map/psum | solution.py:26
  440.6 1.5 fusion.2
  442.2 2.5 convolution_convert_fusion.1
  444.7 1.0 fusion.8
  445.7 20.6 %all-reduce.18.cloned.1.call-done = bf16[256,256]{1,0:T(8,128)(2,1)} async-done(((bf16[256,256]{1,0:T(8,128)(2,1)}), bf16[256,256]{1,0:T(8,128)(2,1)}) %all-reduce.18.cloned.1.call-update) | async-done | bytes 131088 | tf_op jit(solution)/shard_map/psum | solution.py:26
  466.4 1.5 fusion.1
  467.9 2.5 convolution_convert_fusion
  470.5 2.9 fusion.6
  473.4 0.8 copy.14
  474.9 17.2 %all-reduce.20.cloned.1.call-done = bf16[256,256]{1,0:T(8,128)(2,1)} async-done(((bf16[256,256]{1,0:T(8,128)(2,1)}), bf16[256,256]{1,0:T(8,128)(2,1)}) %all-reduce.20.cloned.1.call-update) | async-done | bytes 131088 | tf_op jit(solution)/shard_map/psum | solution.py:26
  492.1 2.5 fusion
  494.6 50.5 %all-gather.5.cloned.1.call-done = bf16[1024,2048]{0,1:T(8,128)(2,1)} async-done(((bf16[1024,128]{0,1:T(8,128)(2,1)}), bf16[1024,2048]{0,1:T(8,128)(2,1)}) %all-gather.5.cloned.1.call-update) | async-done | bytes 4194320 | tf_op jit(solution)/shard_map/all_gather | solution.py:53
  545.1 6.4 %copy.13 = bf16[1024,2048]{1,0:T(8,128)(2,1)} copy(bf16[1024,2048]{0,1:T(8,128)(2,1)} %all-gather.5.cloned.1.call-done) | data formatting | bytes 8388608
  (30 shorter events, 2.3 us)
Async XLA Ops:
  7.2 227.5 %copy-start = (f32[1024,256]{1,0:T(8,128)S(1)}, f32[1024,256]{1,0:T(8,128)}, u32[]{:S(2)}) copy-start(f32[1024,256]{1,0:T(8,128)} %param.9) | copy-start | bytes 3145732
  7.2 109.1 %all-gather.3.cloned.1.call-start = ((), (), s32[]{:S(2)}) async-start(), calls=%async_computation.1 | async-start | bytes 12582912 | tf_op jit(solution)/shard_map/all_gather | solution.py:34
  7.9 226.7 %reduce-scatter.2.cloned.1.call-start = ((), (), s32[]{:S(2)}) async-start(), calls=%async_computation.2 | async-start | bytes 8912896 | tf_op jit(solution)/shard_map/reduce_scatter | solution.py:38
  130.9 127.2 %all-reduce.8.cloned.1.call-start = ((), (), s32[]{:S(2)}) async-start(), calls=%async_computation.3 | async-start | bytes 131072 | tf_op jit(solution)/shard_map/psum | solution.py:39
  237.4 118.5 %all-reduce.10.cloned.1.call-start = ((), (), s32[]{:S(2)}) async-start(), calls=%async_computation.5 | async-start | bytes 2097152 | tf_op jit(solution)/shard_map/psum | solution.py:55
  260.7 128.4 %all-reduce.12.cloned.1.call-start = ((), (), s32[]{:S(2)}) async-start(), calls=%async_computation.6 | async-start | bytes 262144 | tf_op jit(solution)/shard_map/psum | solution.py:26
  355.8 33.3 %copy-start.1 = (f32[1024,256]{1,0:T(8,128)S(1)}, f32[1024,256]{1,0:T(8,128)}, u32[]{:S(2)}) copy-start(f32[1024,256]{1,0:T(8,128)} %all-reduce.10.cloned.1.call-done) | copy-start | bytes 3145732
  368.3 46.6 %all-reduce.14.cloned.1.call-start = ((), (), s32[]{:S(2)}) async-start(), calls=%async_computation.7 | async-start | bytes 262144 | tf_op jit(solution)/shard_map/psum | solution.py:26
  390.7 30.2 %copy-start.2 = (f32[256,128]{1,0:T(8,128)S(1)}, f32[256,128]{1,0:T(8,128)}, u32[]{:S(2)}) copy-start(f32[256,128]{1,0:T(8,128)} %param.10) | copy-start | bytes 393220
  390.7 30.3 %copy-start.3 = (f32[256,128]{1,0:T(8,128)S(1)}, f32[256,128]{1,0:T(8,128)}, u32[]{:S(2)}) copy-start(f32[256,128]{1,0:T(8,128)} %param.11) | copy-start | bytes 393220
  393.2 47.4 %all-reduce.16.cloned.1.call-start = ((), (), s32[]{:S(2)}) async-start(), calls=%async_computation.8 | async-start | bytes 262144 | tf_op jit(solution)/shard_map/psum | solution.py:26
  419.0 47.4 %all-reduce.18.cloned.1.call-start = ((), (), s32[]{:S(2)}) async-start(), calls=%async_computation.9 | async-start | bytes 262144 | tf_op jit(solution)/shard_map/psum | solution.py:26
  444.7 47.4 %all-reduce.20.cloned.1.call-start = ((), (), s32[]{:S(2)}) async-start(), calls=%async_computation.10 | async-start | bytes 262144 | tf_op jit(solution)/shard_map/psum | solution.py:26
  470.4 74.7 %all-gather.5.cloned.1.call-start = ((), (), s32[]{:S(2)}) async-start(), calls=%async_computation.4 | async-start | bytes 4456448 | tf_op jit(solution)/shard_map/all_gather | solution.py:53
Sparse Core Ops, SparseCore 0:
  9.5 106.6 all-gather.2
  131.0 103.5 reduce-scatter.1
  237.5 20.5 all-reduce.7
  262.0 93.7 all-reduce.9
  368.4 20.6 all-reduce.11
  393.4 21.5 all-reduce.13
  419.1 21.5 all-reduce.15
  444.8 21.5 all-reduce.17
  470.5 21.5 all-reduce.19
  494.7 50.3 all-gather.4
where the time goes:
time: 559 us; the launch traced here: 558 us
  waiting for transfers between devices  478 us (86%)
  matrix products  45.4 us (8%)
  between operations  15 us (3%)
  local copies, waits for them, and re-layouts  10.6 us (2%)
    all_gather x1, waiting for transfers between devices, shards(): lax.all_gather(grad_out, 'group', axis=0, tiled=True)  108 us
    reduce_scatter x1, waiting for transfers between devices, shards(): lax.psum_scatter(partial_grad, 'dp', scatter_dimension=1, tiled=True)  104 us
    psum x5, waiting for transfers between devices, refine_group(): lax.psum(inner_gram(iterate).astype(jnp.bfloat16), 'group')  99 us
    psum x1, waiting for transfers between devices, shards(): subspace = lax.psum(subspace_terms, 'dp')  95.1 us
    all_gather x1, waiting for transfers between devices, shards(): new_weight = lax.all_gather(updated, 'dp', axis=1, tiled=True)  50.5 us
    psum x1, waiting for transfers between devices, shards(): lax.psum(matmul(old_basis.T, grad_block).astype(jnp.bfloat16), 'group')  20.7 us
    dot_general x8, matrix products, matmul(): return jnp.dot(left, right, precision=HIGHEST)  16.8 us
    dot_general x1, matrix products, shards(): lax.dot_general(inputs, lax.all_gather(grad_out, 'group', axis=0, tiled=T...  14.6 us
  transfers between devices with their start and end apart: 10, of which 10 were waited for; matrix products, arithmetic and copies ran while one was open for 2% of the time, Pallas kernels for 0%

commit v1 on v0

--- a/solution.py
+++ b/solution.py
@@ -50,7 +50,22 @@
     col_offset = lax.axis_index("dp") * col_count
     own_cols = lax.dynamic_slice_in_dim(weight, col_offset, col_count, 1).astype(jnp.float32)
     updated = (own_cols - matmul(old_basis, direction)).astype(jnp.bfloat16)
-    new_weight = lax.all_gather(updated, "dp", axis=1, tiled=True)
+    ways, here, step = (lax.axis_size("dp"), lax.axis_index("dp"), updated.shape[1])
+    dims = [n * ways if d == 1 else n for d, n in enumerate(updated.shape)]
+    new_weight = lax.dynamic_update_slice_in_dim(
+        jnp.zeros(dims, updated.dtype), updated, here * step, axis=1
+    )
+    going_up = going_down = updated
+    for far in range(1, ways // 2 + 1):
+        going_up = lax.ppermute(going_up, "dp", [(d, (d + 1) % ways) for d in range(ways)])
+        new_weight = lax.dynamic_update_slice_in_dim(
+            new_weight, going_up, (here - far) % ways * step, axis=1
+        )
+        if 2 * far < ways:
+            going_down = lax.ppermute(going_down, "dp", [(d, (d - 1) % ways) for d in range(ways)])
+            new_weight = lax.dynamic_update_slice_in_dim(
+                new_weight, going_down, (here + far) % ways * step, axis=1
+            )
     subspace_terms = matmul(grad_block, projected.T)
     subspace = lax.psum(subspace_terms, "dp")
     new_basis = refine_group(subspace)

time: 559 us -> 524 us (0.937)
  waiting for transfers between devices: 478 us -> 401 us
  starting transfers between devices: 0.59 us -> 28 us
  local copies, waits for them, and re-layouts: 10.6 us -> 26.3 us
    all_gather x1 -> x0, waiting for transfers between devices: 50.5 us -> none  [shards(): new_weight = lax.all_gather(updated, 'dp', axis=1, tiled=True)]
    psum x5, waiting for transfers between devices: 99 us -> 70.1 us  [refine_group(): lax.psum(inner_gram(iterate).astype(jnp.bfloat16), 'group')]
    ppermute x0 -> x15, starting transfers between devices: none -> 27.6 us  [the longest x7 27.2 us: shards(): lax.ppermute(going_down, 'dp', [(d, (d - 1) % ways) for d in range(ways)])]
    dynamic_update_slice x0 -> x16, local copies, waits for them, and re-layouts: none -> 11.6 us  [the longest x8 5.81 us: shards(): lax.dynamic_update_slice_in_dim(new_weight, going_up, (here - far) % ways...]
    ppermute x0 -> x15, local copies, waits for them, and re-layouts: none -> 9.16 us  [the longest x8 5.14 us: shards(): lax.ppermute(going_up, 'dp', [(d, (d + 1) % ways) for d in range(ways)])]
    unnamed x14 -> x13, local copies, waits for them, and re-layouts: 9.66 us -> 1.87 us
    ppermute x0 -> x15, waiting for transfers between devices: none -> 7.39 us  [the longest x8 7.38 us: shards(): lax.ppermute(going_up, 'dp', [(d, (d + 1) % ways) for d in range(ways)])]
  transfers between devices with their start and end apart: 10 -> 24, of which waited for: 10 -> 11; matrix products, arithmetic and copies ran while one was open for 2% -> 10% of each run, Pallas kernels for 0% -> 0%
where the time goes in v1:
time: 524 us; the launch traced here: 523 us
  waiting for transfers between devices  401 us (77%)
  matrix products  44.6 us (9%)
  starting transfers between devices  28 us (5%)
  local copies, waits for them, and re-layouts  26.3 us (5%)
  between operations  15.2 us (3%)
  blocking collectives  5.54 us (1%)
    all_gather x1, waiting for transfers between devices, shards(): lax.all_gather(grad_out, 'group', axis=0, tiled=True)  108 us
    reduce_scatter x1, waiting for transfers between devices, shards(): lax.psum_scatter(partial_grad, 'dp', scatter_dimension=1, tiled=True)  104 us
    psum x1, waiting for transfers between devices, shards(): subspace = lax.psum(subspace_terms, 'dp')  90.5 us
    psum x5, waiting for transfers between devices, refine_group(): lax.psum(inner_gram(iterate).astype(jnp.bfloat16), 'group')  70.1 us
    ppermute x7, starting transfers between devices, shards(): lax.ppermute(going_down, 'dp', [(d, (d - 1) % ways) for d in range(ways)])  27.2 us
    psum x1, waiting for transfers between devices, shards(): lax.psum(matmul(old_basis.T, grad_block).astype(jnp.bfloat16), 'group')  20.7 us
    dot_general x8, matrix products, matmul(): return jnp.dot(left, right, precision=HIGHEST)  15.9 us
    dot_general x1, matrix products, shards(): lax.dot_general(inputs, lax.all_gather(grad_out, 'group', axis=0, tiled=T...  14.6 us
  transfers between devices with their start and end apart: 24, of which 11 were waited for; matrix products, arithmetic and copies ran while one was open for 10% of the time, Pallas kernels for 0%

profile of v1, /device:TPU:0, one launch (start us, length us, event | category | flops | bytes accessed | tf_op | source)
XLA Modules:
  0.0 523.3 jit_solution(14110787422751220477)
XLA Ops:
  8.0 108.3 %all-gather.2.cloned.1.call-done = bf16[2048,2048]{1,0:T(8,128)(2,1)} async-done(((bf16[1024,2048]{1,0:T(8,128)(2,1)}), bf16[2048,2048]{1,0:T(8,128)(2,1)}) %all-gather.2.cloned.1.call-update) | async-done | bytes 8388624 | tf_op jit(solution)/shard_map/all_gather | solution.py:34
  116.3 14.6 %fusion.21 = f32[1024,2048]{1,0:T(8,128)} fusion(bf16[2048,1024]{1,0:T(8,128)(2,1)} %param.6, bf16[2048,2048]{1,0:T(8,128)(2,1)} %all-gather.2.cloned.1.call-done), kind=kOutput, calls=%fused_computation.54 | convolution fusion | flops 8589934592 | bytes 20971520 | tf_op jit(solution)/shard_map/dot_general | solution.py:32
  131.0 103.7 %reduce-scatter.2.cloned.1.call-done = f32[1024,128]{1,0:T(8,128)} async-done(((f32[1024,2048]{1,0:T(8,128)}), f32[1024,128]{1,0:T(8,128)}) %reduce-scatter.2.cloned.1.call-update) | async-done | bytes 524304 | tf_op jit(solution)/shard_map/reduce_scatter | solution.py:38
  234.6 2.7 fusion.7
  237.4 20.7 %all-reduce.8.cloned.1.call-done = bf16[256,128]{0,1:T(8,128)(2,1)} async-done(((bf16[256,128]{0,1:T(8,128)(2,1)}), bf16[256,128]{0,1:T(8,128)(2,1)}) %all-reduce.8.cloned.1.call-update) | async-done | bytes 65552 | tf_op jit(solution)/shard_map/psum | solution.py:39
  258.1 2.6 fusion.22
  263.5 3.3 collective-permute-start.1
  266.7 90.5 %all-reduce.10.cloned.1.call-done = f32[1024,256]{1,0:T(8,128)} async-done(((f32[1024,256]{1,0:T(8,128)}), f32[1024,256]{1,0:T(8,128)}) %all-reduce.10.cloned.1.call-update) | async-done | bytes 1048592 | tf_op jit(solution)/shard_map/psum | solution.py:70
  357.2 2.1 multiply_reduce_fusion
  359.3 5.5 %psum.58 = f32[]{:T(128)} all-reduce(f32[]{:T(128)} %multiply_reduce_fusion), channel_id=1, replica_groups=mesh['dp'=16,'group'=2] {'group'}, use_global_device_ids=true, to_apply=%region_4.5 | all-reduce | flops 1 | bytes 8 | tf_op jit(solution)/shard_map/psum | solution.py:23
  365.6 4.1 convolution_convert_fusion.4
  371.7 2.5 broadcast_in_dim.3
  375.5 4.2 collective-permute-start.3
  379.7 11.7 %all-reduce.12.cloned.1.call-done = bf16[256,256]{1,0:T(8,128)(2,1)} async-done(((bf16[256,256]{1,0:T(8,128)(2,1)}), bf16[256,256]{1,0:T(8,128)(2,1)}) %all-reduce.12.cloned.1.call-update) | async-done | bytes 131088 | tf_op jit(solution)/shard_map/psum | solution.py:26
  391.4 2.3 fusion.4
  393.7 2.5 convolution_convert_fusion.3
  399.1 4.4 collective-permute-start.5
  403.5 14.4 %all-reduce.14.cloned.1.call-done = bf16[256,256]{1,0:T(8,128)(2,1)} async-done(((bf16[256,256]{1,0:T(8,128)(2,1)}), bf16[256,256]{1,0:T(8,128)(2,1)}) %all-reduce.14.cloned.1.call-update) | async-done | bytes 131088 | tf_op jit(solution)/shard_map/psum | solution.py:26
  417.9 1.5 fusion.3
  419.4 2.5 convolution_convert_fusion.2
  425.8 4.4 collective-permute-start.7
  430.2 13.4 %all-reduce.16.cloned.1.call-done = bf16[256,256]{1,0:T(8,128)(2,1)} async-done(((bf16[256,256]{1,0:T(8,128)(2,1)}), bf16[256,256]{1,0:T(8,128)(2,1)}) %all-reduce.16.cloned.1.call-update) | async-done | bytes 131088 | tf_op jit(solution)/shard_map/psum | solution.py:26
  443.6 1.5 fusion.2
  445.1 2.5 convolution_convert_fusion.1
  450.3 3.2 collective-permute-start.9
  453.5 15.8 %all-reduce.18.cloned.1.call-done = bf16[256,256]{1,0:T(8,128)(2,1)} async-done(((bf16[256,256]{1,0:T(8,128)(2,1)}), bf16[256,256]{1,0:T(8,128)(2,1)}) %all-reduce.18.cloned.1.call-update) | async-done | bytes 131088 | tf_op jit(solution)/shard_map/psum | solution.py:26
  470.9 2.5 convolution_convert_fusion
  477.1 3.2 collective-permute-start.11
  480.3 14.8 %all-reduce.20.cloned.1.call-done = bf16[256,256]{1,0:T(8,128)(2,1)} async-done(((bf16[256,256]{1,0:T(8,128)(2,1)}), bf16[256,256]{1,0:T(8,128)(2,1)}) %all-reduce.20.cloned.1.call-update) | async-done | bytes 131088 | tf_op jit(solution)/shard_map/psum | solution.py:26
  495.1 2.5 fusion
  499.7 4.5 collective-permute-start.13
  509.9 6.0 %collective-permute-done.14 = bf16[1024,128]{0,1:T(8,128)(2,1)S(1)} collective-permute-done((bf16[1024,128]{0,1:T(8,128)(2,1)S(1)}, bf16[1024,128]{0,1:T(8,128)(2,1)S(1)}, u32[]{:S(2)}, u32[]{:S(2)}) %collective-permute-start.14) | collective-permute-done | bytes 262176 | tf_op jit(solution)/shard_map/ppermute | solution.py:60
  (89 shorter events, 29.7 us)
Async XLA Ops:
  7.2 227.5 %copy-start = (f32[1024,256]{1,0:T(8,128)S(1)}, f32[1024,256]{1,0:T(8,128)}, u32[]{:S(2)}) copy-start(f32[1024,256]{1,0:T(8,128)} %param.9) | copy-start | bytes 3145732
  7.2 109.1 %all-gather.2.cloned.1.call-start = ((), (), s32[]{:S(2)}) async-start(), calls=%async_computation.1 | async-start | bytes 12582912 | tf_op jit(solution)/shard_map/all_gather | solution.py:34
  7.9 226.7 %reduce-scatter.2.cloned.1.call-start = ((), (), s32[]{:S(2)}) async-start(), calls=%async_computation.2 | async-start | bytes 8912896 | tf_op jit(solution)/shard_map/reduce_scatter | solution.py:38
  130.9 130.9 %copy-start.2 = (f32[256,128]{1,0:T(8,128)S(1)}, f32[256,128]{1,0:T(8,128)}, u32[]{:S(2)}) copy-start(f32[256,128]{1,0:T(8,128)} %param.10) | copy-start | bytes 393220
  130.9 131.0 %copy-start.3 = (f32[256,128]{1,0:T(8,128)S(1)}, f32[256,128]{1,0:T(8,128)}, u32[]{:S(2)}) copy-start(f32[256,128]{1,0:T(8,128)} %param.11) | copy-start | bytes 393220
  130.9 127.2 %all-reduce.8.cloned.1.call-start = ((), (), s32[]{:S(2)}) async-start(), calls=%async_computation.3 | async-start | bytes 131072 | tf_op jit(solution)/shard_map/psum | solution.py:39
  237.4 119.8 %all-reduce.10.cloned.1.call-start = ((), (), s32[]{:S(2)}) async-start(), calls=%async_computation.4 | async-start | bytes 2097152 | tf_op jit(solution)/shard_map/psum | solution.py:70
  258.1 4.1 copy-start.1
  260.7 130.6 %all-reduce.12.cloned.1.call-start = ((), (), s32[]{:S(2)}) async-start(), calls=%async_computation.5 | async-start | bytes 262144 | tf_op jit(solution)/shard_map/psum | solution.py:26
  263.5 112.0 %collective-permute-start.1 = (bf16[1024,128]{0,1:T(8,128)(2,1)S(1)}, bf16[1024,128]{0,1:T(8,128)(2,1)S(1)}, u32[]{:S(2)}, u32[]{:S(2)}) collective-permute-start(bf16[1024,128]{0,1:T(8,128)(2,1)S(1)} %fusion.6), channel_id=1, source_target_pairs={{0,30},{2,0},{4,2},{6,4},{8,6},{10,8},{12,10},{14,12},{16,14},{18,... | collective-permute-start | bytes 786440 | tf_op jit(solution)/shard_map/ppermute | solution.py:65
  359.3 15.7 %collective-permute-start = (bf16[1024,128]{0,1:T(8,128)(2,1)S(1)}, bf16[1024,128]{0,1:T(8,128)(2,1)S(1)}, u32[]{:S(2)}, u32[]{:S(2)}) collective-permute-start(bf16[1024,128]{0,1:T(8,128)(2,1)S(1)} %fusion.6), channel_id=1, source_target_pairs={{0,2},{2,4},{4,6},{6,8},{8,10},{10,12},{12,14},{14,16},{16,18},{18... | collective-permute-start | bytes 786440 | tf_op jit(solution)/shard_map/ppermute | solution.py:60
  369.7 48.2 %all-reduce.14.cloned.1.call-start = ((), (), s32[]{:S(2)}) async-start(), calls=%async_computation.6 | async-start | bytes 262144 | tf_op jit(solution)/shard_map/psum | solution.py:26
  375.2 22.7 %collective-permute-start.2 = (bf16[1024,128]{0,1:T(8,128)(2,1)S(1)}, bf16[1024,128]{0,1:T(8,128)(2,1)}, u32[]{:S(2)}, u32[]{:S(2)}) collective-permute-start(bf16[1024,128]{0,1:T(8,128)(2,1)S(1)} %collective-permute-done), channel_id=1, source_target_pairs={{0,2},{2,4},{4,6},{6,8},{8,10},{10,12},{12,14},{14,16},{16,18},{18... | collective-permute-start | bytes 786440 | tf_op jit(solution)/shard_map/ppermute | solution.py:60
  375.5 23.6 %collective-permute-start.3 = (bf16[1024,128]{0,1:T(8,128)(2,1)S(1)}, bf16[1024,128]{0,1:T(8,128)(2,1)}, u32[]{:S(2)}, u32[]{:S(2)}) collective-permute-start(bf16[1024,128]{0,1:T(8,128)(2,1)S(1)} %collective-permute-done.1), channel_id=1, source_target_pairs={{0,30},{2,0},{4,2},{6,4},{8,6},{10,8},{12,10},{14,12},{16,14},{18,... | collective-permute-start | bytes 786440 | tf_op jit(solution)/shard_map/ppermute | solution.py:65
  396.2 47.4 %all-reduce.16.cloned.1.call-start = ((), (), s32[]{:S(2)}) async-start(), calls=%async_computation.7 | async-start | bytes 262144 | tf_op jit(solution)/shard_map/psum | solution.py:26
  399.0 25.6 %collective-permute-start.4 = (bf16[1024,128]{0,1:T(8,128)(2,1)}, bf16[1024,128]{0,1:T(8,128)(2,1)}, u32[]{:S(2)}, u32[]{:S(2)}) collective-permute-start(bf16[1024,128]{0,1:T(8,128)(2,1)} %collective-permute-done.2), channel_id=1, source_target_pairs={{0,2},{2,4},{4,6},{6,8},{8,10},{10,12},{12,14},{14,16},{16,18},{18... | collective-permute-start | bytes 786440 | tf_op jit(solution)/shard_map/ppermute | solution.py:60
  399.1 26.7 %collective-permute-start.5 = (bf16[1024,128]{0,1:T(8,128)(2,1)}, bf16[1024,128]{0,1:T(8,128)(2,1)}, u32[]{:S(2)}, u32[]{:S(2)}) collective-permute-start(bf16[1024,128]{0,1:T(8,128)(2,1)} %collective-permute-done.3), channel_id=1, source_target_pairs={{0,30},{2,0},{4,2},{6,4},{8,6},{10,8},{12,10},{14,12},{16,14},{18,... | collective-permute-start | bytes 786440 | tf_op jit(solution)/shard_map/ppermute | solution.py:65
  421.9 47.4 %all-reduce.18.cloned.1.call-start = ((), (), s32[]{:S(2)}) async-start(), calls=%async_computation.8 | async-start | bytes 262144 | tf_op jit(solution)/shard_map/psum | solution.py:26
  425.7 27.8 %collective-permute-start.6 = (bf16[1024,128]{0,1:T(8,128)(2,1)}, bf16[1024,128]{0,1:T(8,128)(2,1)}, u32[]{:S(2)}, u32[]{:S(2)}) collective-permute-start(bf16[1024,128]{0,1:T(8,128)(2,1)} %collective-permute-done.4), channel_id=1, source_target_pairs={{0,2},{2,4},{4,6},{6,8},{8,10},{10,12},{12,14},{14,16},{16,18},{18... | collective-permute-start | bytes 786440 | tf_op jit(solution)/shard_map/ppermute | solution.py:60
  425.8 24.5 %collective-permute-start.7 = (bf16[1024,128]{0,1:T(8,128)(2,1)}, bf16[1024,128]{0,1:T(8,128)(2,1)}, u32[]{:S(2)}, u32[]{:S(2)}) collective-permute-start(bf16[1024,128]{0,1:T(8,128)(2,1)} %collective-permute-done.5), channel_id=1, source_target_pairs={{0,30},{2,0},{4,2},{6,4},{8,6},{10,8},{12,10},{14,12},{16,14},{18,... | collective-permute-start | bytes 786440 | tf_op jit(solution)/shard_map/ppermute | solution.py:65
  447.7 47.4 %all-reduce.20.cloned.1.call-start = ((), (), s32[]{:S(2)}) async-start(), calls=%async_computation.9 | async-start | bytes 262144 | tf_op jit(solution)/shard_map/psum | solution.py:26
  450.3 26.8 %collective-permute-start.9 = (bf16[1024,128]{0,1:T(8,128)(2,1)}, bf16[1024,128]{0,1:T(8,128)(2,1)S(1)}, u32[]{:S(2)}, u32[]{:S(2)}) collective-permute-start(bf16[1024,128]{0,1:T(8,128)(2,1)} %collective-permute-done.7), channel_id=1, source_target_pairs={{0,30},{2,0},{4,2},{6,4},{8,6},{10,8},{12,10},{14,12},{16,14},{18,... | collective-permute-start | bytes 786440 | tf_op jit(solution)/shard_map/ppermute | solution.py:65
  453.5 26.8 %collective-permute-start.8 = (bf16[1024,128]{0,1:T(8,128)(2,1)}, bf16[1024,128]{0,1:T(8,128)(2,1)}, u32[]{:S(2)}, u32[]{:S(2)}) collective-permute-start(bf16[1024,128]{0,1:T(8,128)(2,1)} %collective-permute-done.6), channel_id=1, source_target_pairs={{0,2},{2,4},{4,6},{6,8},{8,10},{10,12},{12,14},{14,16},{16,18},{18... | collective-permute-start | bytes 786440 | tf_op jit(solution)/shard_map/ppermute | solution.py:60
  477.1 22.6 %collective-permute-start.11 = (bf16[1024,128]{0,1:T(8,128)(2,1)S(1)}, bf16[1024,128]{0,1:T(8,128)(2,1)S(1)}, u32[]{:S(2)}, u32[]{:S(2)}) collective-permute-start(bf16[1024,128]{0,1:T(8,128)(2,1)S(1)} %collective-permute-done.9), channel_id=1, source_target_pairs={{0,30},{2,0},{4,2},{6,4},{8,6},{10,8},{12,10},{14,12},{16,14},{18,... | collective-permute-start | bytes 786440 | tf_op jit(solution)/shard_map/ppermute | solution.py:65
  480.3 18.4 %collective-permute-start.10 = (bf16[1024,128]{0,1:T(8,128)(2,1)}, bf16[1024,128]{0,1:T(8,128)(2,1)S(1)}, u32[]{:S(2)}, u32[]{:S(2)}) collective-permute-start(bf16[1024,128]{0,1:T(8,128)(2,1)} %collective-permute-done.8), channel_id=1, source_target_pairs={{0,2},{2,4},{4,6},{6,8},{8,10},{10,12},{12,14},{14,16},{16,18},{18... | collective-permute-start | bytes 786440 | tf_op jit(solution)/shard_map/ppermute | solution.py:60
  498.7 8.6 %collective-permute-start.12 = (bf16[1024,128]{0,1:T(8,128)(2,1)S(1)}, bf16[1024,128]{0,1:T(8,128)(2,1)S(1)}, u32[]{:S(2)}, u32[]{:S(2)}) collective-permute-start(bf16[1024,128]{0,1:T(8,128)(2,1)S(1)} %collective-permute-done.10), channel_id=1, source_target_pairs={{0,2},{2,4},{4,6},{6,8},{8,10},{10,12},{12,14},{14,16},{16,18},{18... | collective-permute-start | bytes 786440 | tf_op jit(solution)/shard_map/ppermute | solution.py:60
  499.7 8.6 %collective-permute-start.13 = (bf16[1024,128]{0,1:T(8,128)(2,1)S(1)}, bf16[1024,128]{0,1:T(8,128)(2,1)S(1)}, u32[]{:S(2)}, u32[]{:S(2)}) collective-permute-start(bf16[1024,128]{0,1:T(8,128)(2,1)S(1)} %collective-permute-done.11), channel_id=1, source_target_pairs={{0,30},{2,0},{4,2},{6,4},{8,6},{10,8},{12,10},{14,12},{16,14},{18,... | collective-permute-start | bytes 786440 | tf_op jit(solution)/shard_map/ppermute | solution.py:65
  507.4 8.5 %collective-permute-start.14 = (bf16[1024,128]{0,1:T(8,128)(2,1)S(1)}, bf16[1024,128]{0,1:T(8,128)(2,1)S(1)}, u32[]{:S(2)}, u32[]{:S(2)}) collective-permute-start(bf16[1024,128]{0,1:T(8,128)(2,1)S(1)} %collective-permute-done.12), channel_id=1, source_target_pairs={{0,2},{2,4},{4,6},{6,8},{8,10},{10,12},{12,14},{14,16},{16,18},{18... | collective-permute-start | bytes 786440 | tf_op jit(solution)/shard_map/ppermute | solution.py:60
Sparse Core Ops, SparseCore 0:
  9.5 106.6 all-gather.1
  131.0 103.5 reduce-scatter.1
  237.5 20.5 all-reduce.7
  262.0 95.1 all-reduce.9
  369.8 21.5 all-reduce.11
  396.3 21.5 all-reduce.13
  422.1 21.5 all-reduce.15
  447.8 21.5 all-reduce.17
  473.5 21.5 all-reduce.19
